TPU v7x, 512 devices: a whole 4x8x8 slice. The times are simulated.
512 devices in a mesh: chan: 128 (over z, y, core), tm: 4 (over x).
Axes of the slice: x: 4, y: 8, z: 8, core: 2. Of those that a mesh axis runs over, the one named last changes fastest.
Arguments:
- visibilities: bfloat16 [4, 1024, 16384], P('tm', 'chan'), may hold values from -6 to 6
- flags: int32 [4, 1024, 2048], P('tm', 'chan'), may hold values 0 or 1
- taper: float32 [1024], P('chan'), may hold values from 0.3 to 1
- group_ids: int32 [2048], replicated, may hold values from 0 to 15
Outputs:
- spectrum: float32 [4, 16, 1024], P(None, None, 'chan')
Inputs may be any that keep to these rules, and one draw needn't show every extreme that they name: `group_ids`: each baseline's group number.
All inputs are finite; a program needn't handle non-finite values. No bound on the sum of `flags` on one device may be relied on, other than what follows from the above.
Results may differ from a plain program's by a relative error of at most 0.0051.
Values may be sent and summed in bfloat16 or wider, within the bound.
No kernel may reach another device: no remote copies, remote signals or barrier semaphores. Data moves between devices by JAX's collectives and lax.ppermute only.
A program may use at most 64 MiB of HBM per device.

v0:
```python
import math
import jax
import jax.numpy as jnp
from jax import lax
from jax.sharding import PartitionSpec as P

G = 16


def tables(length):
    positions = jnp.arange(length, dtype=jnp.int32)
    product = positions[:, None] * positions[None, :] % length
    phases = product.astype(jnp.float32) * (2.0 * math.pi / length)
    normalizing_scale = 1.0 / math.sqrt(length)
    return (
        (jnp.cos(phases) * normalizing_scale).astype(jnp.bfloat16),
        (jnp.sin(phases) * normalizing_scale).astype(jnp.bfloat16),
    )


def body(visibilities, flags, taper, group_ids):
    local_times, local_chans, column_entries = visibilities.shape
    baseline_pairs = column_entries // 8
    channels = local_chans * lax.axis_size("chan")
    shard_count = baseline_pairs // lax.axis_size("chan")
    times_all = local_times * lax.axis_size("tm")
    cos_tab, sin_tab = tables(channels)
    group_range = jnp.arange(G, dtype=jnp.int32)
    shard_group_index = lax.dynamic_slice_in_dim(
        group_ids, lax.axis_index("chan") * shard_count, shard_count
    )
    group_member = (shard_group_index[None, :] == group_range[:, None]).astype(jnp.float32)
    turned = lax.all_to_all(visibilities, "chan", split_axis=2, concat_axis=1, tiled=True)
    turned_flags = lax.all_to_all(flags, "chan", split_axis=2, concat_axis=1, tiled=True)
    full_taper = lax.all_gather(taper, "chan", axis=0, tiled=True)
    weight = (1 - turned_flags).astype(jnp.float32) * full_taper[None, :, None]
    shaped = turned.reshape(local_times, channels, shard_count, 8).astype(jnp.float32)
    tapered = (
        (shaped * weight[..., None])
        .astype(jnp.bfloat16)
        .reshape(local_times, channels, shard_count * 8)
    )
    items = tapered.shape[0]
    cosine_part = jnp.einsum(
        "dc,tcn->tdn", cos_tab, tapered, preferred_element_type=jnp.float32
    ).reshape(items, channels, shard_count, 4, 2)
    sine_part = jnp.einsum(
        "dc,tcn->tdn", sin_tab, tapered, preferred_element_type=jnp.float32
    ).reshape(items, channels, shard_count, 4, 2)
    real_part = cosine_part[..., 0] + sine_part[..., 1]
    imag_part = cosine_part[..., 1] - sine_part[..., 0]
    group_real = jnp.einsum(
        "tdbs,gb->tsgd", real_part, group_member, precision=lax.Precision.HIGHEST
    )
    group_imag = jnp.einsum(
        "tdbs,gb->tsgd", imag_part, group_member, precision=lax.Precision.HIGHEST
    )
    autocorrelation_terms = jnp.einsum(
        "tdbs,gb->tsgd",
        real_part * real_part + imag_part * imag_part,
        group_member,
        precision=lax.Precision.HIGHEST,
    )
    group_terms = jnp.stack([group_real, group_imag, autocorrelation_terms], axis=1)
    owned = lax.psum_scatter(group_terms, "chan", scatter_dimension=4, tiled=True)
    spectrum = jnp.sum(owned[:, 0] * owned[:, 0] + owned[:, 1] * owned[:, 1] - owned[:, 2], axis=0)
    spectrum = lax.psum(spectrum, "tm")
    member_all = (group_ids[None, :] == group_range[:, None]).astype(jnp.float32)
    counts = jnp.sum(member_all, axis=1)
    pair_count = jnp.maximum(counts * (counts - 1.0), 1.0)
    return spectrum / jnp.sqrt(pair_count * times_all)[None, :, None]


def solution(mesh):
    return jax.shard_map(
        body,
        mesh=mesh,
        in_specs=(P("tm", "chan", None), P("tm", "chan", None), P("chan"), P()),
        out_specs=P(None, None, "chan"),
        check_vma=False,
    )
```

profile of v0, /device:TPU:24, one launch (start us, length us, event | category | flops | bytes accessed | tf_op | source)
XLA Modules:
  0.0 725.1 jit_solution(13528118081946566250)
XLA Ops:
  6.5 1.9 copy.69
  8.4 0.5 broadcast.92
  8.9 9.3 %reduce = s32[2048,8]{1,0:T(8,128)S(1)} reduce(s32[2048,1,8]{2,1,0:T(1,128)S(1)} %bitcast.79, s32[]{:T(128)} %broadcast.92), dimensions={1}, to_apply=%bitcast.69.reduce_sub_computation | reduce | bytes 131076
  18.3 1.1 reshape.135
  19.4 17.1 %all-to-all-start.1 = ((s32[128,1,128]{2,1,0:T(1,128)}), s32[128,1,128]{2,1,0:T(1,128)S(1)}, u32[]{:S(2)}, u32[]{:S(2)}) async-start(s32[128,1,128]{2,1,0:T(1,128)} %reshape.135), calls=%async_computation.1 | async-start | bytes 131072 | tf_op jit(solution)/shard_map/all_to_all | solution.py:34
  36.6 12.7 %copy.66 = bf16[1,8,16384]{1,0,2:T(2,128)(2,1)} copy(bf16[1,8,16384]{2,1,0:T(8,128)(2,1)S(1)} %copy-done) | data formatting | bytes 524288 | tf_op args[0]
  49.3 0.5 broadcast.94
  49.8 90.8 %reduce.2 = bf16[16384,8]{1,0:T(8,128)(2,1)} reduce(bf16[16384,1,8]{2,1,0:T(2,128)(2,1)} %bitcast.77, bf16[]{:T(256)} %broadcast.94), dimensions={1}, to_apply=%bitcast.71.reduce_sub_computation | reduce | bytes 524290
  140.6 6.9 reshape.137
  147.5 0.6 fusion.48
  149.1 237.0 %all-reduce = f32[1024]{0:T(1024)S(1)} all-reduce(f32[1024]{0:T(1024)S(1)} %dynamic-update-slice), channel_id=1, replica_groups=mesh['chan'=128,'tm'=4] {'chan'}, use_global_device_ids=true, to_apply=%add | all-reduce | flops 1024 | bytes 8192
  386.1 21.1 %all-to-all-start = ((bf16[128,2,512]{2,1,0:T(2,128)(2,1)}), bf16[128,2,512]{2,1,0:T(2,128)(2,1)S(1)}, u32[]{:S(2)}, u32[]{:S(2)}) async-start(bf16[128,2,512]{2,1,0:T(2,128)(2,1)} %reshape.137), calls=%async_computation | async-start | bytes 524288 | tf_op jit(solution)/shard_map/all_to_all | solution.py:33
  407.4 0.8 reduce.1
  408.2 1.6 reshape.136
  409.9 0.5 copy.70
  410.6 0.3 bitcast_multiply_fusion
  411.3 8.6 %all-to-all-done = bf16[128,2,512]{2,1,0:T(2,128)(2,1)S(1)} async-done(((bf16[128,2,512]{2,1,0:T(2,128)(2,1)}), bf16[128,2,512]{2,1,0:T(2,128)(2,1)S(1)}, u32[]{:S(2)}, u32[]{:S(2)}) %all-to-all-start) | async-done | bytes 262176 | tf_op jit(solution)/shard_map/all_to_all | solution.py:33
  420.0 17.1 %reshape.138 = bf16[16384,1,8]{2,1,0:T(2,128)(2,1)} reshape(bf16[128,2,512]{2,1,0:T(2,128)(2,1)S(1)} %all-to-all-done) | data formatting | bytes 524288
  437.1 14.8 %copy.67 = bf16[1,8,16384]{2,1,0:T(8,128)(2,1)S(1)} copy(bf16[1,8,16384]{1,0,2:T(2,128)(2,1)} %bitcast.78) | data formatting | bytes 524288 | tf_op jit(solution)/shard_map/all_to_all | solution.py:33
  452.0 0.3 fusion.14
  452.3 16.1 %fusion.13 = f32[1,1024,128]{1,2,0:T(8,128)S(1)} fusion(bf16[1024,128]{1,0:T(8,128)(2,1)S(1)} %fusion.14), kind=kOutput, calls=%fused_computation.16 | convolution fusion | flops 285212672 | bytes 786432 | tf_op jit(solution)/shard_map/dc,tcn->tdn/dot_general | solution.py:44
  468.4 16.5 %fusion.12 = f32[1,1024,128]{1,2,0:T(8,128)S(1)} fusion(bf16[1024,128]{1,0:T(8,128)(2,1)S(1)} %fusion.14), kind=kOutput, calls=%fused_computation.15 | convolution fusion | flops 285212672 | bytes 786432 | tf_op jit(solution)/shard_map/dc,tcn->tdn/dot_general | solution.py:47
  484.9 0.3 reshape.124
  485.5 1.2 fusion.46
  486.7 0.6 convolution_bitcast_fusion.2
  487.3 1.1 convolution_bitcast_fusion
  488.3 0.6 convolution_bitcast_fusion.1
  489.0 4.6 copy.78
  494.4 205.7 %all-reduce.4.cloned.1.call-done = f32[1,3,4,16,1024]{3,2,1,0,4:T(4,128)} async-done(((f32[1,3,4,16,1024]{3,2,1,0,4:T(4,128)}), f32[1,3,4,16,1024]{3,2,1,0,4:T(4,128)}) %all-reduce.4.cloned.1.call-update) | async-done | bytes 786448
  700.1 0.8 constant_dynamic-slice_fusion.1
  700.9 16.8 %psum.7 = f32[4,16,8]{1,2,0:T(8,128)S(1)} all-reduce(f32[4,16,8]{1,2,0:T(8,128)S(1)} %fusion.24), channel_id=1, replica_groups=mesh['chan'=128,'tm'=4] {'tm'}, use_global_device_ids=true, to_apply=%region_1.2 | all-reduce | flops 512 | bytes 4096 | tf_op jit(solution)/shard_map/psum | solution.py:67
  717.7 0.6 broadcast_divide_fusion
  (26 shorter events, 1.9 us)
Async XLA Ops:
  6.5 30.1 %copy-start = (bf16[1,8,16384]{2,1,0:T(8,128)(2,1)S(1)}, bf16[1,8,16384]{2,1,0:T(8,128)(2,1)}, u32[]{:S(2)}) copy-start(bf16[1,8,16384]{2,1,0:T(8,128)(2,1)} %param.4) | copy-start | bytes 786436
  19.4 366.6 %all-to-all-start.1 = ((s32[128,1,128]{2,1,0:T(1,128)}), s32[128,1,128]{2,1,0:T(1,128)S(1)}, u32[]{:S(2)}, u32[]{:S(2)}) async-start(s32[128,1,128]{2,1,0:T(1,128)} %reshape.135), calls=%async_computation.1 | async-start | bytes 131072 | tf_op jit(solution)/shard_map/all_to_all | solution.py:34
  140.6 6.9 copy-start.2
  140.6 8.2 %copy-start.1 = (s32[2048]{0:T(1024)S(1)}, s32[2048]{0:T(1024)}, u32[]{:S(2)}) copy-start(s32[2048]{0:T(1024)} %param.7) | copy-start | bytes 24580
  140.6 8.3 %copy-start.3 = (f32[8]{0:T(128)S(1)}, f32[8]{0:T(128)}, u32[]{:S(2)}) copy-start(f32[8]{0:T(128)} %param.6) | copy-start | bytes 100
  386.1 33.9 %all-to-all-start = ((bf16[128,2,512]{2,1,0:T(2,128)(2,1)}), bf16[128,2,512]{2,1,0:T(2,128)(2,1)S(1)}, u32[]{:S(2)}, u32[]{:S(2)}) async-start(bf16[128,2,512]{2,1,0:T(2,128)(2,1)} %reshape.137), calls=%async_computation | async-start | bytes 524288 | tf_op jit(solution)/shard_map/all_to_all | solution.py:33
  407.1 292.9 %all-reduce.4.cloned.1.call-start = ((), (), s32[]{:S(2)}) async-start(), calls=%async_computation.2 | async-start | bytes 12582912
Sparse Core Ops, SparseCore 0:
  493.8 206.2 all-reduce.3
where the time goes:
time: 726 us; the launch traced here: 725 us
  blocking collectives  254 us (35%)
  waiting for transfers between devices  214 us (29%)
  other arithmetic  102 us (14%)
  local copies, waits for them, and re-layouts  66.5 us (9%)
  starting transfers between devices  38.5 us (5%)
  matrix products  34.8 us (5%)
  between operations  14.9 us (2%)
    unnamed x1, blocking collectives  237 us
    unnamed x2, waiting for transfers between devices  206 us
    unnamed x3, other arithmetic  100 us
    unnamed x20, local copies, waits for them, and re-layouts  43.4 us
    all_to_all x1, starting transfers between devices, body(): lax.all_to_all(visibilities, 'chan', split_axis=2, concat_axis=1, tiled=T...  21.1 us
    all_to_all x1, starting transfers between devices, body(): lax.all_to_all(flags, 'chan', split_axis=2, concat_axis=1, tiled=True)  17.1 us
    psum x1, blocking collectives, body(): spectrum = lax.psum(spectrum, 'tm')  16.8 us
    dot_general x1, matrix products, body(): jnp.einsum('dc,tcn->tdn', sin_tab, tapered, preferred_element_type=jnp.fl...  16.5 us
  transfers between devices with their start and end apart: 3, of which 2 were waited for; matrix products, arithmetic and copies ran while one was open for 16% of the time, Pallas kernels for 0%

commit v1 on v0

--- a/solution.py
+++ b/solution.py
@@ -30,7 +30,12 @@
         group_ids, lax.axis_index("chan") * shard_count, shard_count
     )
     group_member = (shard_group_index[None, :] == group_range[:, None]).astype(jnp.float32)
-    turned = lax.all_to_all(visibilities, "chan", split_axis=2, concat_axis=1, tiled=True)
+    turned = jnp.concatenate(
+        lax.all_to_all(
+            jnp.stack(jnp.split(visibilities, lax.axis_size("chan"), axis=2)), "chan", 0, 0
+        ),
+        axis=1,
+    )
     turned_flags = lax.all_to_all(flags, "chan", split_axis=2, concat_axis=1, tiled=True)
     full_taper = lax.all_gather(taper, "chan", axis=0, tiled=True)
     weight = (1 - turned_flags).astype(jnp.float32) * full_taper[None, :, None]

time: 726 us -> 665 us (0.916); the launches traced: 725 us -> 656 us
  other arithmetic: 102 us -> 11.3 us
  local copies, waits for them, and re-layouts: 66.5 us -> 89.1 us
    unnamed x3 -> x1, other arithmetic: 100 us -> 9.34 us
    unnamed x20 -> x142, local copies, waits for them, and re-layouts: 43.4 us -> 80 us
    all_to_all x1 -> x0, local copies, waits for them, and re-layouts: 14.8 us -> none  [body(): lax.all_to_all(visibilities, 'chan', split_axis=2, concat_axis=1, tiled=T...]
  transfers between devices with their start and end apart: 3 -> 3, of which waited for: 2 -> 2; matrix products, arithmetic and copies ran while one was open for 16% -> 12% of each run, Pallas kernels for 0% -> 0%
where the time goes in v1:
time: 665 us; the launch traced here: 656 us
  blocking collectives  254 us (38%)
  waiting for transfers between devices  214 us (32%)
  local copies, waits for them, and re-layouts  89.1 us (13%)
  starting transfers between devices  38.2 us (6%)
  matrix products  34.3 us (5%)
  between operations  15.2 us (2%)
  other arithmetic  11.3 us (2%)
    unnamed x1, blocking collectives  237 us
    unnamed x2, waiting for transfers between devices  206 us
    unnamed x142, local copies, waits for them, and re-layouts  80 us
    all_to_all x1, starting transfers between devices, body(): lax.all_to_all(jnp.stack(jnp.split(visibilities, lax.axis_size('chan'), a...  21.1 us
    all_to_all x1, starting transfers between devices, body(): lax.all_to_all(flags, 'chan', split_axis=2, concat_axis=1, tiled=True)  17.1 us
    psum x1, blocking collectives, body(): spectrum = lax.psum(spectrum, 'tm')  16.8 us
    dot_general x1, matrix products, body(): jnp.einsum('dc,tcn->tdn', cos_tab, tapered, preferred_element_type=jnp.fl...  16.1 us
    dot_general x1, matrix products, body(): jnp.einsum('dc,tcn->tdn', sin_tab, tapered, preferred_element_type=jnp.fl...  16 us
  transfers between devices with their start and end apart: 3, of which 2 were waited for; matrix products, arithmetic and copies ran while one was open for 12% of the time, Pallas kernels for 0%

profile of v1, /device:TPU:24, one launch (start us, length us, event | category | flops | bytes accessed | tf_op | source)
XLA Modules:
  0.0 656.3 jit_solution(16165732554115645789)
XLA Ops:
  6.5 1.9 copy.51
  9.0 9.3 %reduce = s32[2048,8]{1,0:T(8,128)S(1)} reduce(s32[2048,1,8]{2,1,0:T(1,128)S(1)} %bitcast.321, s32[]{:T(128)} %broadcast.92), dimensions={1}, to_apply=%bitcast.319.reduce_sub_computation | reduce | bytes 131076
  18.3 1.1 reshape.130
  19.4 17.1 %all-to-all-start.1 = ((s32[128,1,128]{2,1,0:T(1,128)}), s32[128,1,128]{2,1,0:T(1,128)S(1)}, u32[]{:S(2)}, u32[]{:S(2)}) async-start(s32[128,1,128]{2,1,0:T(1,128)} %reshape.130), calls=%async_computation.1 | async-start | bytes 131072 | tf_op jit(solution)/shard_map/all_to_all | solution.py:39
  36.6 0.7 fusion.50
  38.2 237.0 %all-reduce = f32[1024]{0:T(1024)S(1)} all-reduce(f32[1024]{0:T(1024)S(1)} %dynamic-update-slice), channel_id=1, replica_groups=mesh['chan'=128,'tm'=4] {'chan'}, use_global_device_ids=true, to_apply=%add | all-reduce | flops 1024 | bytes 8192
  275.2 0.6 constant_dynamic-update-slice_fusion.127
  282.8 0.6 constant_dynamic-update-slice_fusion.114
  286.9 0.6 constant_dynamic-update-slice_fusion.107
  300.3 0.6 constant_dynamic-update-slice_fusion.84
  303.2 0.6 constant_dynamic-update-slice_fusion.79
  317.2 0.6 constant_dynamic-update-slice_fusion.55
  323.6 0.6 constant_dynamic-update-slice_fusion.44
  328.8 0.6 constant_dynamic-update-slice_fusion.35
  330.0 0.6 constant_dynamic-update-slice_fusion.33
  334.7 0.6 constant_dynamic-update-slice_fusion.25
  341.6 0.6 constant_dynamic-update-slice_fusion.13
  347.4 0.6 constant_dynamic-update-slice_fusion.3
  349.9 21.1 %all-to-all-start = ((bf16[128,1,8,128]{3,2,1,0:T(8,128)(2,1)}), bf16[128,1,8,128]{3,2,1,0:T(8,128)(2,1)S(1)}, u32[]{:S(2)}, u32[]{:S(2)}) async-start(bf16[128,1,8,128]{3,2,1,0:T(8,128)(2,1)} %constant_dynamic-update-slice_fusion), calls=%async_computation | async-start | bytes 524288 | tf_op jit(solution)/shard_map/all_to_all | solution.py:34
  371.0 0.8 reduce.1
  371.8 1.6 reshape.131
  373.4 0.7 copy.52
  375.1 8.7 %all-to-all-done = bf16[128,1,8,128]{3,2,1,0:T(8,128)(2,1)S(1)} async-done(((bf16[128,1,8,128]{3,2,1,0:T(8,128)(2,1)}), bf16[128,1,8,128]{3,2,1,0:T(8,128)(2,1)S(1)}, u32[]{:S(2)}, u32[]{:S(2)}) %all-to-all-start) | async-done | bytes 262176 | tf_op jit(solution)/shard_map/all_to_all | solution.py:34
  383.8 16.1 %fusion.13 = f32[1,1024,128]{1,2,0:T(8,128)S(1)} fusion(f32[1024,128]{1,0:T(8,128)S(1)} %copy.55, bf16[128,1,8,128]{3,2,1,0:T(8,128)(2,1)S(1)} %all-to-all-done), kind=kOutput, calls=%fused_computation.16 | convolution fusion | flops 285605888 | bytes 1310720 | tf_op jit(solution)/shard_map/dc,tcn->tdn/dot_general | solution.py:49
  400.2 16.0 %fusion.12 = f32[1,1024,128]{1,2,0:T(8,128)S(1)} fusion(f32[1024,128]{1,0:T(8,128)S(1)} %copy.55, bf16[128,1,8,128]{3,2,1,0:T(8,128)(2,1)S(1)} %all-to-all-done), kind=kOutput, calls=%fused_computation.15 | convolution fusion | flops 285605888 | bytes 1310720 | tf_op jit(solution)/shard_map/dc,tcn->tdn/dot_general | solution.py:52
  416.5 1.2 fusion.48
  418.2 1.1 convolution_bitcast_fusion
  420.0 4.6 copy.60
  425.4 205.7 %all-reduce.4.cloned.1.call-done = f32[1,3,4,16,1024]{3,2,1,0,4:T(4,128)} async-done(((f32[1,3,4,16,1024]{3,2,1,0,4:T(4,128)}), f32[1,3,4,16,1024]{3,2,1,0,4:T(4,128)}) %all-reduce.4.cloned.1.call-update) | async-done | bytes 786448
  631.0 0.8 constant_dynamic-slice_fusion.1
  631.8 16.8 %psum.7 = f32[4,16,8]{1,2,0:T(8,128)S(1)} all-reduce(f32[4,16,8]{1,2,0:T(8,128)S(1)} %fusion.24), channel_id=1, replica_groups=mesh['chan'=128,'tm'=4] {'tm'}, use_global_device_ids=true, to_apply=%region_1.2 | all-reduce | flops 512 | bytes 4096 | tf_op jit(solution)/shard_map/psum | solution.py:72
  648.6 0.6 broadcast_divide_fusion
  (145 shorter events, 71.2 us)
Async XLA Ops:
  6.5 30.1 %copy-start.2 = (u32[512]{0:T(512)S(1)}, u32[512]{0:T(512)}, u32[]{:S(2)}) copy-start(u32[512]{0:T(512)} %constant.45) | copy-start | bytes 6148
  6.5 31.5 %copy-start.3 = (f32[8]{0:T(128)S(1)}, f32[8]{0:T(128)}, u32[]{:S(2)}) copy-start(f32[8]{0:T(128)} %param.6) | copy-start | bytes 100
  6.5 268.7 %copy-start = (bf16[1,8,16384]{2,1,0:T(8,128)(2,1)S(1)}, bf16[1,8,16384]{2,1,0:T(8,128)(2,1)}, u32[]{:S(2)}) copy-start(bf16[1,8,16384]{2,1,0:T(8,128)(2,1)} %param.4) | copy-start | bytes 786436
  6.5 342.7 %copy-start.1 = (s32[2048]{0:T(1024)S(1)}, s32[2048]{0:T(1024)}, u32[]{:S(2)}) copy-start(s32[2048]{0:T(1024)} %param.7) | copy-start | bytes 24580
  19.4 330.4 %all-to-all-start.1 = ((s32[128,1,128]{2,1,0:T(1,128)}), s32[128,1,128]{2,1,0:T(1,128)S(1)}, u32[]{:S(2)}, u32[]{:S(2)}) async-start(s32[128,1,128]{2,1,0:T(1,128)} %reshape.130), calls=%async_computation.1 | async-start | bytes 131072 | tf_op jit(solution)/shard_map/all_to_all | solution.py:39
  349.9 33.9 %all-to-all-start = ((bf16[128,1,8,128]{3,2,1,0:T(8,128)(2,1)}), bf16[128,1,8,128]{3,2,1,0:T(8,128)(2,1)S(1)}, u32[]{:S(2)}, u32[]{:S(2)}) async-start(bf16[128,1,8,128]{3,2,1,0:T(8,128)(2,1)} %constant_dynamic-update-slice_fusion), calls=%async_computation | async-start | bytes 524288 | tf_op jit(solution)/shard_map/all_to_all | solution.py:34
  370.9 260.1 %all-reduce.4.cloned.1.call-start = ((), (), s32[]{:S(2)}) async-start(), calls=%async_computation.2 | async-start | bytes 12582912
Sparse Core Ops, SparseCore 0:
  424.7 206.2 all-reduce.3
